TPU v7x, 128 devices: a whole 4x4x4 slice. The times are simulated.
128 devices in a mesh: region: 8 (over x, core), unit: 16 (over y, z).
Axes of the slice: x: 4, y: 4, z: 4, core: 2. Of those that a mesh axis runs over, the one named last changes fastest.
Arguments:
- noisy: bfloat16 [32768, 2048], P(('region', 'unit')), may hold values from -6 to 6
- strategy: bfloat16 [2048, 2048], replicated, may hold values from -0.125 to 0.125
- county_hist: float32 [1024, 2048], P(('region', 'unit')), may hold values from -24 to 24
- tract_county: int32 [32768], P(('region', 'unit')), may hold values from 0 to 1023, as said below
- tract_owner: int32 [32768, 1], P(('region', 'unit')), may hold values from 0 to 127; in each aligned block of 256 rows (0 to 255, 256 to 511, ...) at most 4 rows name the same one
Outputs:
- released: bfloat16 [32768, 2048], P(('region', 'unit'))
- relaid: float32 [65536, 2048], P(('region', 'unit'))
Inputs may be any that keep to these rules, and one draw needn't show every extreme that they name: `tract_county`: every county has at least one tract; the tracts of region r (rows r * 256 * 16 onward) lie in counties of region r (rows r * 8 * 16 onward of county_hist). `tract_owner`: among the 256 rows of one device no owner appears more than 4 times, and some owner appears exactly 4 times.
All inputs are finite; a program needn't handle non-finite values.
Results may differ from a plain program's by a relative error of at most 0.005.
Values sent between devices are 32-bit elements; how exact they have to be, the bound alone decides.
No kernel may reach another device: no remote copies, remote signals or barrier semaphores. Data moves between devices by JAX's collectives and lax.ppermute only.
A program may use at most 64 MiB of HBM per device.

v0:
```python
import jax
import jax.numpy as jnp
from jax import lax
from jax.sharding import PartitionSpec as P

ITERS = 2
step_size = 0.25


def local(noisy, strategy, county_hist, tract_county, tract_owner):
    unit_count = lax.axis_size("unit")
    region_count = lax.axis_size("region")
    devices = region_count * unit_count
    tract_rows = noisy.shape[0]
    width = strategy.shape[0]
    county_region = county_hist.shape[0] * unit_count
    first_county = lax.axis_index("region") * county_region
    local_id = tract_county - first_county
    member = (local_id[:, None] == jnp.arange(county_region, dtype=jnp.int32)[None, :]).astype(
        jnp.float32
    )
    county_tally = jnp.sum(member, axis=0)
    estimate = jnp.zeros((tract_rows, width), jnp.float32)
    for iteration in range(ITERS):
        if iteration == 0:
            misfit = -noisy
        else:
            answers = jnp.dot(
                estimate.astype(jnp.bfloat16), strategy, preferred_element_type=jnp.float32
            )
            misfit = (answers - noisy.astype(jnp.float32)).astype(jnp.bfloat16)
        gradient = lax.dot_general(
            misfit, strategy, (((1,), (1,)), ((), ())), preferred_element_type=jnp.float32
        )
        stepped = estimate - step_size * gradient
        partial_value = lax.dot_general(
            member,
            stepped,
            (((0,), (0,)), ((), ())),
            precision=lax.Precision.HIGHEST,
            preferred_element_type=jnp.float32,
        )
        child_total, tract_count = (
            lax.psum_scatter(partial_value, "unit", scatter_dimension=0, tiled=True),
            lax.psum_scatter(county_tally, "unit", scatter_dimension=0, tiled=True),
        )
        parent_gap = (county_hist - child_total) / tract_count[:, None]
        region_gap = lax.all_gather(parent_gap, "unit", axis=0, tiled=True)
        estimate = stepped + jnp.dot(
            member, region_gap, precision=lax.Precision.HIGHEST, preferred_element_type=jnp.float32
        )
    owners = tract_owner[:, 0]
    owner_hits = (owners[:, None] == jnp.arange(devices, dtype=jnp.int32)[None, :]).astype(
        jnp.int32
    )
    slot_index = jnp.sum((jnp.cumsum(owner_hits, axis=0) - owner_hits) * owner_hits, axis=1)
    capacity = 2 * tract_rows // devices
    target = owners * capacity + slot_index
    outgoing = jnp.zeros((devices * capacity, width), jnp.float32).at[target].set(estimate)
    released = jnp.dot(
        estimate.astype(jnp.bfloat16), strategy, preferred_element_type=jnp.float32
    ).astype(jnp.bfloat16)
    grouped = outgoing.reshape(devices, capacity, width)
    arrived = lax.all_to_all(grouped, ("region", "unit"), split_axis=0, concat_axis=0, tiled=True)
    relaid = arrived.reshape(devices * capacity, width)
    return (released, relaid)


def solution(mesh):
    in_specs = (
        P(("region", "unit"), None),
        P(),
        P(("region", "unit"), None),
        P(("region", "unit")),
        P(("region", "unit"), None),
    )
    out_specs = (P(("region", "unit"), None), P(("region", "unit"), None))
    return jax.shard_map(local, mesh=mesh, in_specs=in_specs, out_specs=out_specs, check_vma=False)
```

profile of v0, /device:TPU:6, one launch (start us, length us, event | category | flops | bytes accessed | tf_op | source)
XLA Modules:
  0.0 385.6 jit_solution(13782813712799772541)
XLA Ops:
  7.2 0.7 broadcast_subtract_fusion
  7.9 6.1 %fusion = f32[256,2048]{1,0:T(8,128)S(1)} fusion(bf16[2048,2048]{1,0:T(8,128)(2,1)} %param.6, bf16[256,2048]{1,0:T(8,128)(2,1)} %param.5), kind=kOutput, calls=%fused_computation.5 | convolution fusion | flops 2149056512 | bytes 11534336 | tf_op jit(solution)/shard_map/dot_general | solution.py:32
  14.0 1.9 fusion.15
  16.0 0.6 dynamic-slice
  17.4 42.1 %all-reduce.1 = f32[128]{0:T(128)S(1)} all-reduce(f32[128]{0:T(128)S(1)} %convert_reduce_fusion), channel_id=3, replica_groups=mesh['region'=8,'unit'=16] {'unit'}, use_global_device_ids=true, to_apply=%region_2.0.clone | all-reduce | flops 128 | bytes 1024
  59.5 46.5 %all-reduce.6.cloned.1.call-done = f32[128,2048]{1,0:T(8,128)} async-done(((f32[128,2048]{1,0:T(8,128)}), f32[128,2048]{1,0:T(8,128)}) %all-reduce.6.cloned.1.call-update) | async-done | bytes 1048592
  106.0 1.5 fusion.17
  107.6 42.9 %all-gather.3.cloned.1.call-done = f32[128,2048]{1,0:T(8,128)} async-done(((f32[8,2048]{1,0:T(8,128)}), f32[128,2048]{1,0:T(8,128)}) %all-gather.3.cloned.1.call-update) | async-done | bytes 1048592 | tf_op jit(solution)/shard_map/all_gather | solution.py:48
  150.5 3.6 convolution_add_fusion.1
  154.1 11.5 %fusion.1 = f32[256,2048]{1,0:T(8,128)S(1)} fusion(f32[256,2048]{1,0:T(8,128)} %convolution_add_fusion.1, bf16[2048,2048]{1,0:T(8,128)(2,1)} %param.6, bf16[256,2048]{1,0:T(8,128)(2,1)S(1)} %copy-done.3), kind=kOutput, calls=%fused_computation.6 | convolution fusion | flops 4298113024 | bytes 13631488 | tf_op jit(solution)/shard_map/dot_general | solution.py:32
  165.6 1.9 fusion.14
  167.5 0.2 all-gather.5.cloned.1.call-start
  167.7 86.7 %all-reduce.8.cloned.1.call-done = f32[128,2048]{1,0:T(8,128)} async-done(((f32[128,2048]{1,0:T(8,128)}), f32[128,2048]{1,0:T(8,128)}) %all-reduce.8.cloned.1.call-update) | async-done | bytes 1048592
  254.4 1.5 fusion.16
  256.1 0.2 fusion.10
  256.4 0.2 fusion.12
  256.6 42.2 %all-gather.5.cloned.1.call-done = f32[128,2048]{1,0:T(8,128)} async-done(((f32[8,2048]{1,0:T(8,128)}), f32[128,2048]{1,0:T(8,128)}) %all-gather.5.cloned.1.call-update) | async-done | bytes 1048592 | tf_op jit(solution)/shard_map/all_gather | solution.py:48
  298.8 3.6 convolution_add_fusion
  302.4 5.1 %scatter_custom_fusion = f32[512,2048]{1,0:T(8,128)} fusion(s32[256]{0:T(256)S(1)} %bitcast.33, f32[256,2048]{1,0:T(8,128)} %convolution_add_fusion, f32[]{:T(128)} %constant.8.clone.1), kind=kCustom, calls=%fused_computation.10 | custom fusion | bytes 4194816 | tf_op jit(solution)/shard_map/scatter | solution.py:59
  307.6 5.2 %reshape.30 = f32[128,4,2048]{2,1,0:T(4,128)} reshape(f32[512,2048]{1,0:T(8,128)} %scatter_custom_fusion) | data formatting | bytes 8388608 | tf_op jit(solution)/shard_map/reshape | solution.py:63
  312.7 7.8 %all-to-all-start = ((f32[128,4,2048]{2,1,0:T(4,128)}), f32[128,4,2048]{2,1,0:T(4,128)}, u32[]{:S(2)}, u32[]{:S(2)}) async-start(f32[128,4,2048]{2,1,0:T(4,128)} %reshape.30), calls=%async_computation | async-start | bytes 8388608 | tf_op jit(solution)/shard_map/all_to_all | solution.py:64
  320.6 6.7 %convolution_convert_fusion = bf16[256,2048]{1,0:T(8,128)(2,1)} fusion(bf16[2048,2048]{1,0:T(8,128)(2,1)} %param.6, f32[256,2048]{1,0:T(8,128)S(1)} %copy-done), kind=kOutput, calls=%fused_computation.9 | convolution fusion | flops 2148532224 | bytes 11534336 | tf_op jit(solution)/shard_map/dot_general | solution.py:60
  327.3 46.5 %all-to-all-done = f32[128,4,2048]{2,1,0:T(4,128)} async-done(((f32[128,4,2048]{2,1,0:T(4,128)}), f32[128,4,2048]{2,1,0:T(4,128)}, u32[]{:S(2)}, u32[]{:S(2)}) %all-to-all-start) | async-done | bytes 4194336 | tf_op jit(solution)/shard_map/all_to_all | solution.py:64
  373.8 5.3 %reshape.31 = f32[512,2048]{1,0:T(8,128)} reshape(f32[128,4,2048]{2,1,0:T(4,128)} %all-to-all-done) | data formatting | bytes 8388608 | tf_op jit(solution)/shard_map/reshape | solution.py:65
  (27 shorter events, 0.6 us)
Async XLA Ops:
  7.2 98.8 %all-reduce.6.cloned.1.call-start = ((), (), s32[]{:S(2)}) async-start(), calls=%async_computation.3 | async-start | bytes 2097152
  14.0 2.0 copy-start.4
  14.0 92.0 %copy-start.1 = (f32[8,2048]{1,0:T(8,128)S(1)}, f32[8,2048]{1,0:T(8,128)}, u32[]{:S(2)}) copy-start(f32[8,2048]{1,0:T(8,128)} %param.7) | copy-start | bytes 196612
  15.9 134.5 %all-gather.3.cloned.1.call-start = ((), (), s32[]{:S(2)}) async-start(), calls=%async_computation.1 | async-start | bytes 1114112 | tf_op jit(solution)/shard_map/all_gather | solution.py:48
  107.5 46.5 %copy-start.3 = (bf16[256,2048]{1,0:T(8,128)(2,1)S(1)}, bf16[256,2048]{1,0:T(8,128)(2,1)}, u32[]{:S(2)}) copy-start(bf16[256,2048]{1,0:T(8,128)(2,1)} %param.5) | copy-start | bytes 3145732
  107.5 146.9 %all-reduce.8.cloned.1.call-start = ((), (), s32[]{:S(2)}) async-start(), calls=%async_computation.4 | async-start | bytes 2097152
  165.6 90.4 %copy-start.2 = (s32[256,1]{0,1:T(1,128)S(1)}, s32[256,1]{0,1:T(1,128)}, u32[]{:S(2)}) copy-start(s32[256,1]{0,1:T(1,128)} %param.9) | copy-start | bytes 3076
  167.5 131.3 %all-gather.5.cloned.1.call-start = ((), (), s32[]{:S(2)}) async-start(), calls=%async_computation.2 | async-start | bytes 1114112 | tf_op jit(solution)/shard_map/all_gather | solution.py:48
  312.7 7.9 %copy-start = (f32[256,2048]{1,0:T(8,128)S(1)}, f32[256,2048]{1,0:T(8,128)}, u32[]{:S(2)}) copy-start(f32[256,2048]{1,0:T(8,128)} %convolution_add_fusion) | copy-start | bytes 6291460
  312.7 61.1 %all-to-all-start = ((f32[128,4,2048]{2,1,0:T(4,128)}), f32[128,4,2048]{2,1,0:T(4,128)}, u32[]{:S(2)}, u32[]{:S(2)}) async-start(f32[128,4,2048]{2,1,0:T(4,128)} %reshape.30), calls=%async_computation | async-start | bytes 8388608 | tf_op jit(solution)/shard_map/all_to_all | solution.py:64
Sparse Core Ops, SparseCore 0:
  16.1 89.8 all-reduce.5
  108.7 41.7 all-gather.2
  167.6 86.7 all-reduce.7
  257.0 41.7 all-gather.4
where the time goes:
time: 386 us
  waiting for transfers between devices  265 us (69%)
  blocking collectives  42.1 us (11%)
  matrix products  35.3 us (9%)
  local copies, waits for them, and re-layouts  16.4 us (4%)
  between operations  14.5 us (4%)
  starting transfers between devices  8.19 us (2%)
  other arithmetic  4.33 us (1%)
    unnamed x6, waiting for transfers between devices  133 us
    all_gather x2, waiting for transfers between devices, local(): region_gap = lax.all_gather(parent_gap, 'unit', axis=0, tiled=True)  85.1 us
    all_to_all x1, waiting for transfers between devices, local(): lax.all_to_all(grouped, ('region', 'unit'), split_axis=0, concat_axis=0,...  46.5 us
    unnamed x1, blocking collectives  42.1 us
    dot_general x2, matrix products, local(): lax.dot_general(misfit, strategy, (((1,), (1,)), ((), ())), preferred_ele...  17.6 us
    all_to_all x1, starting transfers between devices, local(): lax.all_to_all(grouped, ('region', 'unit'), split_axis=0, concat_axis=0,...  7.85 us
  transfers between devices with their start and end apart: 5, of which 5 were waited for; matrix products, arithmetic and copies ran while one was open for 2% of the time, Pallas kernels for 0%

commit v1 on v0

--- a/solution.py
+++ b/solution.py
@@ -5,6 +5,19 @@
 
 ITERS = 2
 step_size = 0.25
+
+
+def gather_around(x, axis, dim):
+    ways = lax.axis_size(axis)
+    up = [(d, (d + 1) % ways) for d in range(ways)]
+    down = [(d, (d - 1) % ways) for d in range(ways)]
+    earlier, later = ([x], [x])
+    for _ in range(ways // 2):
+        earlier.append(lax.ppermute(earlier[-1], axis, up))
+    for _ in range((ways - 1) // 2):
+        later.append(lax.ppermute(later[-1], axis, down))
+    line = jnp.concatenate([*earlier[::-1], *later[1:]], axis=dim)
+    return jnp.roll(line, (lax.axis_index(axis) - ways // 2) * x.shape[dim], axis=dim)
 
 
 def local(noisy, strategy, county_hist, tract_county, tract_owner):
@@ -45,7 +58,7 @@
             lax.psum_scatter(county_tally, "unit", scatter_dimension=0, tiled=True),
         )
         parent_gap = (county_hist - child_total) / tract_count[:, None]
-        region_gap = lax.all_gather(parent_gap, "unit", axis=0, tiled=True)
+        region_gap = gather_around(parent_gap, "unit", 0)
         estimate = stepped + jnp.dot(
             member, region_gap, precision=lax.Precision.HIGHEST, preferred_element_type=jnp.float32
         )

time: 386 us -> 424 us (1.098)
  starting transfers between devices: 8.19 us -> 89.6 us
  waiting for transfers between devices: 265 us -> 224 us
    all_gather x2 -> x0, waiting for transfers between devices: 85.1 us -> none  [local(): region_gap = lax.all_gather(parent_gap, 'unit', axis=0, tiled=True)]
    ppermute x0 -> x30, starting transfers between devices: none -> 79.6 us  [the longest x14 77.5 us: gather_around(): later.append(lax.ppermute(later[-1], axis, down))]
    ppermute x0 -> x30, waiting for transfers between devices: none -> 41.8 us  [the longest x16 41.3 us: gather_around(): earlier.append(lax.ppermute(earlier[-1], axis, up))]
    unnamed x6 -> x4, waiting for transfers between devices: 133 us -> 135 us
  transfers between devices with their start and end apart: 5 -> 33, of which waited for: 5 -> 23; matrix products, arithmetic and copies ran while one was open for 2% -> 2% of each run, Pallas kernels for 0% -> 0%
where the time goes in v1:
time: 424 us; the launch traced here: 423 us
  waiting for transfers between devices  224 us (53%)
  starting transfers between devices  89.6 us (21%)
  blocking collectives  42.1 us (10%)
  matrix products  33.3 us (8%)
  local copies, waits for them, and re-layouts  16.7 us (4%)
  between operations  15.1 us (4%)
    unnamed x4, waiting for transfers between devices  135 us
    ppermute x14, starting transfers between devices, gather_around(): later.append(lax.ppermute(later[-1], axis, down))  77.5 us
    all_to_all x1, waiting for transfers between devices, local(): lax.all_to_all(grouped, ('region', 'unit'), split_axis=0, concat_axis=0,...  46.5 us
    unnamed x1, blocking collectives  42.1 us
    ppermute x16, waiting for transfers between devices, gather_around(): earlier.append(lax.ppermute(earlier[-1], axis, up))  41.3 us
    dot_general x2, matrix products, local(): lax.dot_general(misfit, strategy, (((1,), (1,)), ((), ())), preferred_ele...  17.8 us
    all_to_all x1, starting transfers between devices, local(): lax.all_to_all(grouped, ('region', 'unit'), split_axis=0, concat_axis=0,...  9.96 us
  transfers between devices with their start and end apart: 33, of which 23 were waited for; matrix products, arithmetic and copies ran while one was open for 2% of the time, Pallas kernels for 0%

profile of v1, /device:TPU:6, one launch (start us, length us, event | category | flops | bytes accessed | tf_op | source)
XLA Modules:
  0.0 423.3 jit_solution(3994232389900689146)
XLA Ops:
  7.9 6.1 %fusion = f32[256,2048]{1,0:T(8,128)S(1)} fusion(bf16[2048,2048]{1,0:T(8,128)(2,1)} %param.8, bf16[256,2048]{1,0:T(8,128)(2,1)} %param.7), kind=kOutput, calls=%fused_computation.5 | convolution fusion | flops 2149056512 | bytes 11534336 | tf_op jit(solution)/shard_map/dot_general | solution.py:45
  17.4 42.1 %all-reduce.1 = f32[128]{0:T(128)S(1)} all-reduce(f32[128]{0:T(128)S(1)} %convert_reduce_fusion), channel_id=3, replica_groups=mesh['region'=8,'unit'=16] {'unit'}, use_global_device_ids=true, to_apply=%region_2.0.clone | all-reduce | flops 128 | bytes 1024
  59.5 46.5 %all-reduce.6.cloned.1.call-done = f32[128,2048]{1,0:T(8,128)} async-done(((f32[128,2048]{1,0:T(8,128)}), f32[128,2048]{1,0:T(8,128)}) %all-reduce.6.cloned.1.call-update) | async-done | bytes 1048592
  107.9 6.6 %collective-permute-done = f32[8,2048]{1,0:T(8,128)S(1)} collective-permute-done((f32[8,2048]{1,0:T(8,128)S(1)}, f32[8,2048]{1,0:T(8,128)S(1)}, u32[]{:S(2)}, u32[]{:S(2)}) %collective-permute-start) | collective-permute-done | bytes 65568 | tf_op jit(solution)/shard_map/ppermute | solution.py:16
  114.5 5.3 %collective-permute-start.8 = (f32[8,2048]{1,0:T(8,128)S(1)}, f32[8,2048]{1,0:T(8,128)S(1)}, u32[]{:S(2)}, u32[]{:S(2)}) collective-permute-start(f32[8,2048]{1,0:T(8,128)S(1)} %fusion.21), channel_id=1, source_target_pairs={{0,15},{1,0},{2,1},{3,2},{4,3},{5,4},{6,5},{7,6},{8,7},{9,8},{10,9... | collective-permute-start | bytes 196616 | tf_op jit(solution)/shard_map/ppermute | solution.py:18
  122.1 5.3 %collective-permute-start.9 = (f32[8,2048]{1,0:T(8,128)S(1)}, f32[8,2048]{1,0:T(8,128)S(1)}, u32[]{:S(2)}, u32[]{:S(2)}) collective-permute-start(f32[8,2048]{1,0:T(8,128)S(1)} %collective-permute-done.8), channel_id=1, source_target_pairs={{0,15},{1,0},{2,1},{3,2},{4,3},{5,4},{6,5},{7,6},{8,7},{9,8},{10,9... | collective-permute-start | bytes 196616 | tf_op jit(solution)/shard_map/ppermute | solution.py:18
  129.6 5.3 %collective-permute-start.10 = (f32[8,2048]{1,0:T(8,128)S(1)}, f32[8,2048]{1,0:T(8,128)S(1)}, u32[]{:S(2)}, u32[]{:S(2)}) collective-permute-start(f32[8,2048]{1,0:T(8,128)S(1)} %collective-permute-done.9), channel_id=1, source_target_pairs={{0,15},{1,0},{2,1},{3,2},{4,3},{5,4},{6,5},{7,6},{8,7},{9,8},{10,9... | collective-permute-start | bytes 196616 | tf_op jit(solution)/shard_map/ppermute | solution.py:18
  137.5 5.6 %collective-permute-start.11 = (f32[8,2048]{1,0:T(8,128)S(1)}, f32[8,2048]{1,0:T(8,128)S(1)}, u32[]{:S(2)}, u32[]{:S(2)}) collective-permute-start(f32[8,2048]{1,0:T(8,128)S(1)} %collective-permute-done.10), channel_id=1, source_target_pairs={{0,15},{1,0},{2,1},{3,2},{4,3},{5,4},{6,5},{7,6},{8,7},{9,8},{10,9... | collective-permute-start | bytes 196616 | tf_op jit(solution)/shard_map/ppermute | solution.py:18
  145.1 5.6 %collective-permute-start.12 = (f32[8,2048]{1,0:T(8,128)S(1)}, f32[8,2048]{1,0:T(8,128)S(1)}, u32[]{:S(2)}, u32[]{:S(2)}) collective-permute-start(f32[8,2048]{1,0:T(8,128)S(1)} %collective-permute-done.11), channel_id=1, source_target_pairs={{0,15},{1,0},{2,1},{3,2},{4,3},{5,4},{6,5},{7,6},{8,7},{9,8},{10,9... | collective-permute-start | bytes 196616 | tf_op jit(solution)/shard_map/ppermute | solution.py:18
  152.7 5.6 %collective-permute-start.13 = (f32[8,2048]{1,0:T(8,128)S(1)}, f32[8,2048]{1,0:T(8,128)S(1)}, u32[]{:S(2)}, u32[]{:S(2)}) collective-permute-start(f32[8,2048]{1,0:T(8,128)S(1)} %collective-permute-done.12), channel_id=1, source_target_pairs={{0,15},{1,0},{2,1},{3,2},{4,3},{5,4},{6,5},{7,6},{8,7},{9,8},{10,9... | collective-permute-start | bytes 196616 | tf_op jit(solution)/shard_map/ppermute | solution.py:18
  160.3 5.6 %collective-permute-start.14 = (f32[8,2048]{1,0:T(8,128)S(1)}, f32[8,2048]{1,0:T(8,128)S(1)}, u32[]{:S(2)}, u32[]{:S(2)}) collective-permute-start(f32[8,2048]{1,0:T(8,128)S(1)} %collective-permute-done.13), channel_id=1, source_target_pairs={{0,15},{1,0},{2,1},{3,2},{4,3},{5,4},{6,5},{7,6},{8,7},{9,8},{10,9... | collective-permute-start | bytes 196616 | tf_op jit(solution)/shard_map/ppermute | solution.py:18
  170.5 11.8 %fusion.1 = f32[256,2048]{1,0:T(8,128)S(1)} fusion(f32[256,2048]{1,0:T(8,128)} %convolution_add_fusion.1, bf16[2048,2048]{1,0:T(8,128)(2,1)} %param.8, bf16[256,2048]{1,0:T(8,128)(2,1)} %param.7), kind=kOutput, calls=%fused_computation.6 | convolution fusion | flops 4298113024 | bytes 13631488 | tf_op jit(solution)/shard_map/dot_general | solution.py:45
  184.3 88.8 %all-reduce.8.cloned.1.call-done = f32[128,2048]{1,0:T(8,128)} async-done(((f32[128,2048]{1,0:T(8,128)}), f32[128,2048]{1,0:T(8,128)}) %all-reduce.8.cloned.1.call-update) | async-done | bytes 1048592
  274.9 6.6 %collective-permute-done.15 = f32[8,2048]{1,0:T(8,128)S(1)} collective-permute-done((f32[8,2048]{1,0:T(8,128)S(1)}, f32[8,2048]{1,0:T(8,128)S(1)}, u32[]{:S(2)}, u32[]{:S(2)}) %collective-permute-start.15) | collective-permute-done | bytes 65568 | tf_op jit(solution)/shard_map/ppermute | solution.py:16
  281.5 5.3 %collective-permute-start.23 = (f32[8,2048]{1,0:T(8,128)S(1)}, f32[8,2048]{1,0:T(8,128)S(1)}, u32[]{:S(2)}, u32[]{:S(2)}) collective-permute-start(f32[8,2048]{1,0:T(8,128)S(1)} %fusion.20), channel_id=1, source_target_pairs={{0,15},{1,0},{2,1},{3,2},{4,3},{5,4},{6,5},{7,6},{8,7},{9,8},{10,9... | collective-permute-start | bytes 196616 | tf_op jit(solution)/shard_map/ppermute | solution.py:18
  289.2 5.4 %collective-permute-start.24 = (f32[8,2048]{1,0:T(8,128)S(1)}, f32[8,2048]{1,0:T(8,128)S(1)}, u32[]{:S(2)}, u32[]{:S(2)}) collective-permute-start(f32[8,2048]{1,0:T(8,128)S(1)} %collective-permute-done.23), channel_id=1, source_target_pairs={{0,15},{1,0},{2,1},{3,2},{4,3},{5,4},{6,5},{7,6},{8,7},{9,8},{10,9... | collective-permute-start | bytes 196616 | tf_op jit(solution)/shard_map/ppermute | solution.py:18
  296.9 5.4 %collective-permute-start.25 = (f32[8,2048]{1,0:T(8,128)S(1)}, f32[8,2048]{1,0:T(8,128)S(1)}, u32[]{:S(2)}, u32[]{:S(2)}) collective-permute-start(f32[8,2048]{1,0:T(8,128)S(1)} %collective-permute-done.24), channel_id=1, source_target_pairs={{0,15},{1,0},{2,1},{3,2},{4,3},{5,4},{6,5},{7,6},{8,7},{9,8},{10,9... | collective-permute-start | bytes 196616 | tf_op jit(solution)/shard_map/ppermute | solution.py:18
  304.7 5.8 %collective-permute-start.26 = (f32[8,2048]{1,0:T(8,128)S(1)}, f32[8,2048]{1,0:T(8,128)S(1)}, u32[]{:S(2)}, u32[]{:S(2)}) collective-permute-start(f32[8,2048]{1,0:T(8,128)S(1)} %collective-permute-done.25), channel_id=1, source_target_pairs={{0,15},{1,0},{2,1},{3,2},{4,3},{5,4},{6,5},{7,6},{8,7},{9,8},{10,9... | collective-permute-start | bytes 196616 | tf_op jit(solution)/shard_map/ppermute | solution.py:18
  312.4 5.7 %collective-permute-start.27 = (f32[8,2048]{1,0:T(8,128)S(1)}, f32[8,2048]{1,0:T(8,128)S(1)}, u32[]{:S(2)}, u32[]{:S(2)}) collective-permute-start(f32[8,2048]{1,0:T(8,128)S(1)} %collective-permute-done.26), channel_id=1, source_target_pairs={{0,15},{1,0},{2,1},{3,2},{4,3},{5,4},{6,5},{7,6},{8,7},{9,8},{10,9... | collective-permute-start | bytes 196616 | tf_op jit(solution)/shard_map/ppermute | solution.py:18
  320.0 5.7 %collective-permute-start.28 = (f32[8,2048]{1,0:T(8,128)S(1)}, f32[8,2048]{1,0:T(8,128)S(1)}, u32[]{:S(2)}, u32[]{:S(2)}) collective-permute-start(f32[8,2048]{1,0:T(8,128)S(1)} %collective-permute-done.27), channel_id=1, source_target_pairs={{0,15},{1,0},{2,1},{3,2},{4,3},{5,4},{6,5},{7,6},{8,7},{9,8},{10,9... | collective-permute-start | bytes 196616 | tf_op jit(solution)/shard_map/ppermute | solution.py:18
  327.6 5.7 %collective-permute-start.29 = (f32[8,2048]{1,0:T(8,128)S(1)}, f32[8,2048]{1,0:T(8,128)S(1)}, u32[]{:S(2)}, u32[]{:S(2)}) collective-permute-start(f32[8,2048]{1,0:T(8,128)S(1)} %collective-permute-done.28), channel_id=1, source_target_pairs={{0,15},{1,0},{2,1},{3,2},{4,3},{5,4},{6,5},{7,6},{8,7},{9,8},{10,9... | collective-permute-start | bytes 196616 | tf_op jit(solution)/shard_map/ppermute | solution.py:18
  348.0 10.0 %all-to-all-start = ((f32[128,4,2048]{2,1,0:T(4,128)}), f32[128,4,2048]{2,1,0:T(4,128)}, u32[]{:S(2)}, u32[]{:S(2)}) async-start(f32[128,4,2048]{2,1,0:T(4,128)} %reshape.30), calls=%async_computation | async-start | bytes 8388608 | tf_op jit(solution)/shard_map/all_to_all | solution.py:77
  358.0 6.7 %convolution_convert_fusion = bf16[256,2048]{1,0:T(8,128)(2,1)} fusion(bf16[2048,2048]{1,0:T(8,128)(2,1)} %param.8, f32[256,2048]{1,0:T(8,128)S(1)} %copy-done), kind=kOutput, calls=%fused_computation.9 | convolution fusion | flops 2148532224 | bytes 11534336 | tf_op jit(solution)/shard_map/dot_general | solution.py:73
  364.7 46.5 %all-to-all-done = f32[128,4,2048]{2,1,0:T(4,128)} async-done(((f32[128,4,2048]{2,1,0:T(4,128)}), f32[128,4,2048]{2,1,0:T(4,128)}, u32[]{:S(2)}, u32[]{:S(2)}) %all-to-all-start) | async-done | bytes 4194336 | tf_op jit(solution)/shard_map/all_to_all | solution.py:77
  (111 shorter events, 59.3 us)
Async XLA Ops:
  7.2 98.8 %all-reduce.6.cloned.1.call-start = ((), (), s32[]{:S(2)}) async-start(), calls=%async_computation.1 | async-start | bytes 2097152
  15.9 257.1 %all-reduce.8.cloned.1.call-start = ((), (), s32[]{:S(2)}) async-start(), calls=%async_computation.2 | async-start | bytes 2097152
  106.9 7.6 %collective-permute-start = (f32[8,2048]{1,0:T(8,128)S(1)}, f32[8,2048]{1,0:T(8,128)S(1)}, u32[]{:S(2)}, u32[]{:S(2)}) collective-permute-start(f32[8,2048]{1,0:T(8,128)S(1)} %fusion.21), channel_id=1, source_target_pairs={{0,1},{1,2},{2,3},{3,4},{4,5},{5,6},{6,7},{7,8},{8,9},{9,10},{10,1... | collective-permute-start | bytes 196616 | tf_op jit(solution)/shard_map/ppermute | solution.py:16
  114.5 7.6 %collective-permute-start.1 = (f32[8,2048]{1,0:T(8,128)S(1)}, f32[8,2048]{1,0:T(8,128)S(1)}, u32[]{:S(2)}, u32[]{:S(2)}) collective-permute-start(f32[8,2048]{1,0:T(8,128)S(1)} %collective-permute-done), channel_id=1, source_target_pairs={{0,1},{1,2},{2,3},{3,4},{4,5},{5,6},{6,7},{7,8},{8,9},{9,10},{10,1... | collective-permute-start | bytes 196616 | tf_op jit(solution)/shard_map/ppermute | solution.py:16
  114.5 7.6 %collective-permute-start.8 = (f32[8,2048]{1,0:T(8,128)S(1)}, f32[8,2048]{1,0:T(8,128)S(1)}, u32[]{:S(2)}, u32[]{:S(2)}) collective-permute-start(f32[8,2048]{1,0:T(8,128)S(1)} %fusion.21), channel_id=1, source_target_pairs={{0,15},{1,0},{2,1},{3,2},{4,3},{5,4},{6,5},{7,6},{8,7},{9,8},{10,9... | collective-permute-start | bytes 196616 | tf_op jit(solution)/shard_map/ppermute | solution.py:18
  129.6 7.9 %collective-permute-start.3 = (f32[8,2048]{1,0:T(8,128)S(1)}, f32[8,2048]{1,0:T(8,128)S(1)}, u32[]{:S(2)}, u32[]{:S(2)}) collective-permute-start(f32[8,2048]{1,0:T(8,128)S(1)} %collective-permute-done.2), channel_id=1, source_target_pairs={{0,1},{1,2},{2,3},{3,4},{4,5},{5,6},{6,7},{7,8},{8,9},{9,10},{10,1... | collective-permute-start | bytes 196616 | tf_op jit(solution)/shard_map/ppermute | solution.py:16
  129.6 7.9 %collective-permute-start.10 = (f32[8,2048]{1,0:T(8,128)S(1)}, f32[8,2048]{1,0:T(8,128)S(1)}, u32[]{:S(2)}, u32[]{:S(2)}) collective-permute-start(f32[8,2048]{1,0:T(8,128)S(1)} %collective-permute-done.9), channel_id=1, source_target_pairs={{0,15},{1,0},{2,1},{3,2},{4,3},{5,4},{6,5},{7,6},{8,7},{9,8},{10,9... | collective-permute-start | bytes 196616 | tf_op jit(solution)/shard_map/ppermute | solution.py:18
  137.5 7.6 %collective-permute-start.11 = (f32[8,2048]{1,0:T(8,128)S(1)}, f32[8,2048]{1,0:T(8,128)S(1)}, u32[]{:S(2)}, u32[]{:S(2)}) collective-permute-start(f32[8,2048]{1,0:T(8,128)S(1)} %collective-permute-done.10), channel_id=1, source_target_pairs={{0,15},{1,0},{2,1},{3,2},{4,3},{5,4},{6,5},{7,6},{8,7},{9,8},{10,9... | collective-permute-start | bytes 196616 | tf_op jit(solution)/shard_map/ppermute | solution.py:18
  145.1 7.6 %collective-permute-start.5 = (f32[8,2048]{1,0:T(8,128)S(1)}, f32[8,2048]{1,0:T(8,128)S(1)}, u32[]{:S(2)}, u32[]{:S(2)}) collective-permute-start(f32[8,2048]{1,0:T(8,128)S(1)} %collective-permute-done.4), channel_id=1, source_target_pairs={{0,1},{1,2},{2,3},{3,4},{4,5},{5,6},{6,7},{7,8},{8,9},{9,10},{10,1... | collective-permute-start | bytes 196616 | tf_op jit(solution)/shard_map/ppermute | solution.py:16
  145.1 7.6 %collective-permute-start.12 = (f32[8,2048]{1,0:T(8,128)S(1)}, f32[8,2048]{1,0:T(8,128)S(1)}, u32[]{:S(2)}, u32[]{:S(2)}) collective-permute-start(f32[8,2048]{1,0:T(8,128)S(1)} %collective-permute-done.11), channel_id=1, source_target_pairs={{0,15},{1,0},{2,1},{3,2},{4,3},{5,4},{6,5},{7,6},{8,7},{9,8},{10,9... | collective-permute-start | bytes 196616 | tf_op jit(solution)/shard_map/ppermute | solution.py:18
  152.7 7.6 %collective-permute-start.6 = (f32[8,2048]{1,0:T(8,128)S(1)}, f32[8,2048]{1,0:T(8,128)S(1)}, u32[]{:S(2)}, u32[]{:S(2)}) collective-permute-start(f32[8,2048]{1,0:T(8,128)S(1)} %collective-permute-done.5), channel_id=1, source_target_pairs={{0,1},{1,2},{2,3},{3,4},{4,5},{5,6},{6,7},{7,8},{8,9},{9,10},{10,1... | collective-permute-start | bytes 196616 | tf_op jit(solution)/shard_map/ppermute | solution.py:16
  160.3 7.8 %collective-permute-start.14 = (f32[8,2048]{1,0:T(8,128)S(1)}, f32[8,2048]{1,0:T(8,128)S(1)}, u32[]{:S(2)}, u32[]{:S(2)}) collective-permute-start(f32[8,2048]{1,0:T(8,128)S(1)} %collective-permute-done.13), channel_id=1, source_target_pairs={{0,15},{1,0},{2,1},{3,2},{4,3},{5,4},{6,5},{7,6},{8,7},{9,8},{10,9... | collective-permute-start | bytes 196616 | tf_op jit(solution)/shard_map/ppermute | solution.py:18
  273.9 7.6 %collective-permute-start.15 = (f32[8,2048]{1,0:T(8,128)S(1)}, f32[8,2048]{1,0:T(8,128)S(1)}, u32[]{:S(2)}, u32[]{:S(2)}) collective-permute-start(f32[8,2048]{1,0:T(8,128)S(1)} %fusion.20), channel_id=1, source_target_pairs={{0,1},{1,2},{2,3},{3,4},{4,5},{5,6},{6,7},{7,8},{8,9},{9,10},{10,1... | collective-permute-start | bytes 196616 | tf_op jit(solution)/shard_map/ppermute | solution.py:16
  281.5 7.6 %collective-permute-start.16 = (f32[8,2048]{1,0:T(8,128)S(1)}, f32[8,2048]{1,0:T(8,128)S(1)}, u32[]{:S(2)}, u32[]{:S(2)}) collective-permute-start(f32[8,2048]{1,0:T(8,128)S(1)} %collective-permute-done.15), channel_id=1, source_target_pairs={{0,1},{1,2},{2,3},{3,4},{4,5},{5,6},{6,7},{7,8},{8,9},{9,10},{10,1... | collective-permute-start | bytes 196616 | tf_op jit(solution)/shard_map/ppermute | solution.py:16
  281.5 7.7 %collective-permute-start.23 = (f32[8,2048]{1,0:T(8,128)S(1)}, f32[8,2048]{1,0:T(8,128)S(1)}, u32[]{:S(2)}, u32[]{:S(2)}) collective-permute-start(f32[8,2048]{1,0:T(8,128)S(1)} %fusion.20), channel_id=1, source_target_pairs={{0,15},{1,0},{2,1},{3,2},{4,3},{5,4},{6,5},{7,6},{8,7},{9,8},{10,9... | collective-permute-start | bytes 196616 | tf_op jit(solution)/shard_map/ppermute | solution.py:18
  289.1 7.6 %collective-permute-start.17 = (f32[8,2048]{1,0:T(8,128)S(1)}, f32[8,2048]{1,0:T(8,128)S(1)}, u32[]{:S(2)}, u32[]{:S(2)}) collective-permute-start(f32[8,2048]{1,0:T(8,128)S(1)} %collective-permute-done.16), channel_id=1, source_target_pairs={{0,1},{1,2},{2,3},{3,4},{4,5},{5,6},{6,7},{7,8},{8,9},{9,10},{10,1... | collective-permute-start | bytes 196616 | tf_op jit(solution)/shard_map/ppermute | solution.py:16
  289.2 7.7 %collective-permute-start.24 = (f32[8,2048]{1,0:T(8,128)S(1)}, f32[8,2048]{1,0:T(8,128)S(1)}, u32[]{:S(2)}, u32[]{:S(2)}) collective-permute-start(f32[8,2048]{1,0:T(8,128)S(1)} %collective-permute-done.23), channel_id=1, source_target_pairs={{0,15},{1,0},{2,1},{3,2},{4,3},{5,4},{6,5},{7,6},{8,7},{9,8},{10,9... | collective-permute-start | bytes 196616 | tf_op jit(solution)/shard_map/ppermute | solution.py:18
  296.7 7.9 %collective-permute-start.18 = (f32[8,2048]{1,0:T(8,128)S(1)}, f32[8,2048]{1,0:T(8,128)S(1)}, u32[]{:S(2)}, u32[]{:S(2)}) collective-permute-start(f32[8,2048]{1,0:T(8,128)S(1)} %collective-permute-done.17), channel_id=1, source_target_pairs={{0,1},{1,2},{2,3},{3,4},{4,5},{5,6},{6,7},{7,8},{8,9},{9,10},{10,1... | collective-permute-start | bytes 196616 | tf_op jit(solution)/shard_map/ppermute | solution.py:16
  296.9 7.8 %collective-permute-start.25 = (f32[8,2048]{1,0:T(8,128)S(1)}, f32[8,2048]{1,0:T(8,128)S(1)}, u32[]{:S(2)}, u32[]{:S(2)}) collective-permute-start(f32[8,2048]{1,0:T(8,128)S(1)} %collective-permute-done.24), channel_id=1, source_target_pairs={{0,15},{1,0},{2,1},{3,2},{4,3},{5,4},{6,5},{7,6},{8,7},{9,8},{10,9... | collective-permute-start | bytes 196616 | tf_op jit(solution)/shard_map/ppermute | solution.py:18
  304.7 7.7 %collective-permute-start.26 = (f32[8,2048]{1,0:T(8,128)S(1)}, f32[8,2048]{1,0:T(8,128)S(1)}, u32[]{:S(2)}, u32[]{:S(2)}) collective-permute-start(f32[8,2048]{1,0:T(8,128)S(1)} %collective-permute-done.25), channel_id=1, source_target_pairs={{0,15},{1,0},{2,1},{3,2},{4,3},{5,4},{6,5},{7,6},{8,7},{9,8},{10,9... | collective-permute-start | bytes 196616 | tf_op jit(solution)/shard_map/ppermute | solution.py:18
  319.8 7.6 %collective-permute-start.21 = (f32[8,2048]{1,0:T(8,128)S(1)}, f32[8,2048]{1,0:T(8,128)S(1)}, u32[]{:S(2)}, u32[]{:S(2)}) collective-permute-start(f32[8,2048]{1,0:T(8,128)S(1)} %collective-permute-done.20), channel_id=1, source_target_pairs={{0,1},{1,2},{2,3},{3,4},{4,5},{5,6},{6,7},{7,8},{8,9},{9,10},{10,1... | collective-permute-start | bytes 196616 | tf_op jit(solution)/shard_map/ppermute | solution.py:16
  327.4 7.6 %collective-permute-start.22 = (f32[8,2048]{1,0:T(8,128)S(1)}, f32[8,2048]{1,0:T(8,128)S(1)}, u32[]{:S(2)}, u32[]{:S(2)}) collective-permute-start(f32[8,2048]{1,0:T(8,128)S(1)} %collective-permute-done.21), channel_id=1, source_target_pairs={{0,1},{1,2},{2,3},{3,4},{4,5},{5,6},{6,7},{7,8},{8,9},{9,10},{10,1... | collective-permute-start | bytes 196616 | tf_op jit(solution)/shard_map/ppermute | solution.py:16
  327.6 7.6 %collective-permute-start.29 = (f32[8,2048]{1,0:T(8,128)S(1)}, f32[8,2048]{1,0:T(8,128)S(1)}, u32[]{:S(2)}, u32[]{:S(2)}) collective-permute-start(f32[8,2048]{1,0:T(8,128)S(1)} %collective-permute-done.28), channel_id=1, source_target_pairs={{0,15},{1,0},{2,1},{3,2},{4,3},{5,4},{6,5},{7,6},{8,7},{9,8},{10,9... | collective-permute-start | bytes 196616 | tf_op jit(solution)/shard_map/ppermute | solution.py:18
  348.0 63.2 %all-to-all-start = ((f32[128,4,2048]{2,1,0:T(4,128)}), f32[128,4,2048]{2,1,0:T(4,128)}, u32[]{:S(2)}, u32[]{:S(2)}) async-start(f32[128,4,2048]{2,1,0:T(4,128)} %reshape.30), calls=%async_computation | async-start | bytes 8388608 | tf_op jit(solution)/shard_map/all_to_all | solution.py:77
  (13 other events, 279.0 us)
Sparse Core Ops, SparseCore 0:
  16.1 89.8 all-reduce.5
  184.4 88.5 all-reduce.7
